TPU v7x, 256 devices: a whole 4x4x8 slice. The times are simulated.
256 devices in a mesh: gx: 32 (over x, y, core), gy: 8 (over z).
Axes of the slice: x: 4, y: 4, z: 8, core: 2. Of those that a mesh axis runs over, the one named last changes fastest.
Arguments:
- leaf_load: bfloat16 [65536, 384], P(('gx', 'gy')), may hold values from -6 to 6
- front_zero: bfloat16 [65536, 8192], P(('gx', 'gy')), may hold values from -0.046875 to 0.046875
- front_one: bfloat16 [32768, 8192], P(('gx', 'gy')), may hold values from -0.046875 to 0.046875
- front_two: bfloat16 [16384, 8192], P(('gx', 'gy')), may hold values from -0.046875 to 0.046875
- front_root: bfloat16 [8192, 8192], P(('gx', 'gy')), may hold values from -0.046875 to 0.046875
- load_one: float32 [32768, 384], P(('gx', 'gy')), may hold values from -6 to 6
- load_two: float32 [16384, 384], P(('gx', 'gy')), may hold values from -6 to 6
- load_root: float32 [8192, 384], P(('gx', 'gy')), may hold values from -6 to 6
- map_one: int32 [8192, 2], replicated, may hold values from 0 to 255
- map_two: int32 [8192, 2], replicated, may hold values from 0 to 127
- map_root: int32 [8192, 2], replicated, may hold values from 0 to 63
- adjoint: float32 [64, 128, 384], P('gx', 'gy'), may hold values from -6 to 6
Outputs:
- root_solution: float32 [8192, 384], P(('gx', 'gy'))
- gradient: float32 [64, 128, 384], P('gx', 'gy')
All inputs are finite; a program needn't handle non-finite values.
Results may differ from a plain program's by a relative error of at most 0.0055.
Values may be sent and summed in bfloat16 or wider, within the bound.
No kernel may reach another device: no remote copies, remote signals or barrier semaphores. Data moves between devices by JAX's collectives and lax.ppermute only.
A program may use at most 64 MiB of HBM per device.

v0:
```python
import jax
import jax.numpy as jnp
from jax import lax
from jax.sharding import PartitionSpec as P


def swapped(x, axis, distance):
    return lax.ppermute(x, axis, [(i, i ^ 1 << distance) for i in range(lax.axis_size(axis))])


def padded_2(cells, sides, width):
    for axis, dim in sides:
        count = lax.axis_size(axis)
        ends = count - 1
        head = lax.slice_in_dim(cells, 0, width, axis=dim)
        tail = lax.slice_in_dim(cells, cells.shape[dim] - width, cells.shape[dim], axis=dim)
        cells = jnp.concatenate(
            [
                lax.ppermute(tail, axis, [(i, (i + 1) % count) for i in range(ends)]),
                cells,
                lax.ppermute(head, axis, [((i + 1) % count, i) for i in range(ends)]),
            ],
            axis=dim,
        )
    return cells


def group_rows(values, bits):
    values = lax.all_gather(values, "gy", axis=0, tiled=True)
    column = lax.axis_index("gx")
    for bit in range(bits):
        other = swapped(values, "gx", bit)
        upper = column >> bit & 1 == 1
        values = jnp.where(
            upper, jnp.concatenate([other, values], 0), jnp.concatenate([values, other], 0)
        )
    return values


def local(
    leaf_load,
    front_zero,
    front_one,
    front_two,
    front_root,
    load_one,
    load_two,
    load_root,
    map_one,
    map_two,
    map_root,
    adjoint,
):
    leaf_bits = lax.axis_size("gx").bit_length() - 4
    fronts = (front_zero, front_one, front_two)
    loads = (load_one, load_two, load_root)
    mappings = (map_one, map_two, map_root)
    column = lax.axis_index("gx")
    row_index = lax.axis_index("gy")
    state = leaf_load
    for level in range(3):
        bits = leaf_bits + level
        whole = group_rows(state, bits)
        product = jnp.dot(fronts[level], whole, preferred_element_type=jnp.float32)
        other = swapped(product, "gx", bits)
        upper = column >> bits & 1 == 1
        first = jnp.where(upper, other, product)
        second = jnp.where(upper, product, other)
        half = product.shape[0] // 2
        position = column % 2 ** (bits + 1) * lax.axis_size("gy") + row_index
        local_map = lax.dynamic_slice_in_dim(mappings[level], position * half, half, 0)
        total = (
            loads[level]
            + jnp.take(first, local_map[:, 0], axis=0)
            + jnp.take(second, local_map[:, 1], axis=0)
        )
        state = total.astype(jnp.bfloat16)
    whole = group_rows(state, leaf_bits + 3)
    root_solution = jnp.dot(front_root, whole, preferred_element_type=jnp.float32)
    cells_x = adjoint.shape[0]
    cells_y = adjoint.shape[1]
    width = adjoint.shape[2]
    plane = root_solution.reshape(cells_x, cells_y, width)
    stacked = jnp.stack([plane, adjoint])
    padded = padded_2(stacked, (("gx", 1), ("gy", 2)), 1)
    padded_u = padded[0]
    padded_a = padded[1]
    gradient = jnp.zeros((cells_x, cells_y, width), jnp.float32)
    for lo_x, lo_y in ((2, 1), (0, 1), (1, 2), (1, 0)):
        near_u = padded_u[lo_x : lo_x + cells_x, lo_y : lo_y + cells_y]
        near_a = padded_a[lo_x : lo_x + cells_x, lo_y : lo_y + cells_y]
        gradient = gradient + (plane - near_u) * (adjoint - near_a)
    return (root_solution, gradient)


def solution(mesh):
    in_specs = (
        P(("gx", "gy"), None),
        P(("gx", "gy"), None),
        P(("gx", "gy"), None),
        P(("gx", "gy"), None),
        P(("gx", "gy"), None),
        P(("gx", "gy"), None),
        P(("gx", "gy"), None),
        P(("gx", "gy"), None),
        P(),
        P(),
        P(),
        P("gx", "gy", None),
    )
    out_specs = (P(("gx", "gy"), None), P("gx", "gy", None))
    return jax.shard_map(local, mesh=mesh, in_specs=in_specs, out_specs=out_specs, check_vma=False)
```

profile of v0, /device:TPU:34, one launch (start us, length us, event | category | flops | bytes accessed | tf_op | source)
XLA Modules:
  0.0 686.3 jit_solution(2727871176709467057)
XLA Ops:
  7.9 44.2 %all-gather.2.cloned.1.call-done = bf16[2048,384]{1,0:T(8,128)(2,1)} async-done(((bf16[256,384]{1,0:T(8,128)(2,1)}), bf16[2048,384]{1,0:T(8,128)(2,1)}) %all-gather.2.cloned.1.call-update) | async-done | bytes 1572880 | tf_op jit(solution)/shard_map/all_gather | solution.py:29
  55.8 5.5 maximum_select_fusion.8
  62.8 69.0 %collective-permute-done.1 = bf16[4096,384]{1,0:T(8,128)(2,1)} collective-permute-done((bf16[4096,384]{1,0:T(8,128)(2,1)}, bf16[4096,384]{1,0:T(8,128)(2,1)}, u32[]{:S(2)}, u32[]{:S(2)}) %collective-permute-start.1) | collective-permute-done | bytes 3145760 | tf_op jit(solution)/shard_map/ppermute | solution.py:8
  131.8 9.1 %fusion.28 = f32[256,384]{0,1:T(8,128)S(1)} fusion(bf16[256,8192]{1,0:T(8,128)(2,1)} %param.19, bf16[4096,384]{1,0:T(8,128)(2,1)} %maximum_select_fusion.8, bf16[4096,384]{1,0:T(8,128)(2,1)} %collective-permute-done.1, pred[]{:T(512)S(6)} %eq.17), kind=kOutput, calls=%fused_computation.45 | convolution fusion | flops 1638924288 | bytes 10878977 | tf_op jit(solution)/shard_map/dot_general | solution.py:64
  144.7 8.1 %collective-permute-done.2 = f32[256,384]{0,1:T(8,128)S(1)} collective-permute-done((f32[256,384]{0,1:T(8,128)S(1)}, f32[256,384]{0,1:T(8,128)S(1)}, u32[]{:S(2)}, u32[]{:S(2)}) %collective-permute-start.2) | collective-permute-done | bytes 393248 | tf_op jit(solution)/shard_map/ppermute | solution.py:8
  154.8 25.7 %all_gather.13 = bf16[1024,384]{1,0:T(8,128)(2,1)S(1)} all-gather(bf16[128,384]{1,0:T(8,128)(2,1)S(1)} %fusion.31), channel_id=1, replica_groups=mesh['gx'=32,'gy'=8] {'gy'}, dimensions={0}, use_global_device_ids=true | all-gather | bytes 884736 | tf_op jit(solution)/shard_map/all_gather | solution.py:29
  184.8 35.0 %collective-permute-done.4 = bf16[2048,384]{1,0:T(8,128)(2,1)S(1)} collective-permute-done((bf16[2048,384]{1,0:T(8,128)(2,1)S(1)}, bf16[2048,384]{1,0:T(8,128)(2,1)S(1)}, u32[]{:S(2)}, u32[]{:S(2)}) %collective-permute-start.4) | collective-permute-done | bytes 1572896 | tf_op jit(solution)/shard_map/ppermute | solution.py:8
  219.8 8.3 %maximum_select_fusion.9 = bf16[4096,384]{1,0:T(8,128)(2,1)} fusion(bf16[2048,384]{1,0:T(8,128)(2,1)S(1)} %maximum_select_fusion.12, bf16[2048,384]{1,0:T(8,128)(2,1)S(1)} %collective-permute-done.4, pred[]{:T(512)S(6)} %eq.17), kind=kLoop, calls=%fused_computation.39 | loop fusion | flops 14155776 | bytes 6291457 | tf_op jit(solution)/shard_map/jit(_where)/select_n | solution.py:34
  231.8 67.4 %collective-permute-done.5 = bf16[4096,384]{1,0:T(8,128)(2,1)} collective-permute-done((bf16[4096,384]{1,0:T(8,128)(2,1)}, bf16[4096,384]{1,0:T(8,128)(2,1)}, u32[]{:S(2)}, u32[]{:S(2)}) %collective-permute-start.5) | collective-permute-done | bytes 3145760 | tf_op jit(solution)/shard_map/ppermute | solution.py:8
  299.2 6.3 fusion.29
  306.4 5.1 collective-permute-done.6
  313.2 25.2 %all_gather.14 = bf16[512,384]{1,0:T(8,128)(2,1)S(1)} all-gather(bf16[64,384]{1,0:T(8,128)(2,1)S(1)} %fusion.32), channel_id=1, replica_groups=mesh['gx'=32,'gy'=8] {'gy'}, dimensions={0}, use_global_device_ids=true | all-gather | bytes 442368 | tf_op jit(solution)/shard_map/all_gather | solution.py:29
  342.0 18.1 %collective-permute-done.8 = bf16[1024,384]{1,0:T(8,128)(2,1)S(1)} collective-permute-done((bf16[1024,384]{1,0:T(8,128)(2,1)S(1)}, bf16[1024,384]{1,0:T(8,128)(2,1)S(1)}, u32[]{:S(2)}, u32[]{:S(2)}) %collective-permute-start.8) | collective-permute-done | bytes 786464 | tf_op jit(solution)/shard_map/ppermute | solution.py:8
  363.6 34.1 %collective-permute-done.9 = bf16[2048,384]{1,0:T(8,128)(2,1)S(1)} collective-permute-done((bf16[2048,384]{1,0:T(8,128)(2,1)S(1)}, bf16[2048,384]{1,0:T(8,128)(2,1)S(1)}, u32[]{:S(2)}, u32[]{:S(2)}) %collective-permute-start.9) | collective-permute-done | bytes 1572896 | tf_op jit(solution)/shard_map/ppermute | solution.py:8
  397.7 8.3 %maximum_select_fusion.10 = bf16[4096,384]{1,0:T(8,128)(2,1)} fusion(bf16[2048,384]{1,0:T(8,128)(2,1)S(1)} %maximum_select_fusion.13, bf16[2048,384]{1,0:T(8,128)(2,1)S(1)} %collective-permute-done.9, pred[]{:T(512)S(6)} %eq.16), kind=kLoop, calls=%fused_computation.40 | loop fusion | flops 14155776 | bytes 6291457 | tf_op jit(solution)/shard_map/jit(_where)/select_n | solution.py:34
  407.3 67.4 %collective-permute-done.10 = bf16[4096,384]{1,0:T(8,128)(2,1)} collective-permute-done((bf16[4096,384]{1,0:T(8,128)(2,1)}, bf16[4096,384]{1,0:T(8,128)(2,1)}, u32[]{:S(2)}, u32[]{:S(2)}) %collective-permute-start.10) | collective-permute-done | bytes 3145760 | tf_op jit(solution)/shard_map/ppermute | solution.py:8
  474.7 6.2 fusion.30
  488.5 24.8 %all_gather.15 = bf16[256,384]{1,0:T(8,128)(2,1)S(1)} all-gather(bf16[32,384]{1,0:T(8,128)(2,1)S(1)} %fusion.41), channel_id=1, replica_groups=mesh['gx'=32,'gy'=8] {'gy'}, dimensions={0}, use_global_device_ids=true | all-gather | bytes 221184 | tf_op jit(solution)/shard_map/all_gather | solution.py:29
  516.4 9.7 %collective-permute-done.13 = bf16[512,384]{1,0:T(8,128)(2,1)S(1)} collective-permute-done((bf16[512,384]{1,0:T(8,128)(2,1)S(1)}, bf16[512,384]{1,0:T(8,128)(2,1)S(1)}, u32[]{:S(2)}, u32[]{:S(2)}) %collective-permute-start.13) | collective-permute-done | bytes 393248 | tf_op jit(solution)/shard_map/ppermute | solution.py:8
  529.5 17.2 %collective-permute-done.14 = bf16[1024,384]{1,0:T(8,128)(2,1)S(1)} collective-permute-done((bf16[1024,384]{1,0:T(8,128)(2,1)S(1)}, bf16[1024,384]{1,0:T(8,128)(2,1)S(1)}, u32[]{:S(2)}, u32[]{:S(2)}) %collective-permute-start.14) | collective-permute-done | bytes 786464 | tf_op jit(solution)/shard_map/ppermute | solution.py:8
  548.1 34.1 %collective-permute-done.15 = bf16[2048,384]{1,0:T(8,128)(2,1)S(1)} collective-permute-done((bf16[2048,384]{1,0:T(8,128)(2,1)S(1)}, bf16[2048,384]{1,0:T(8,128)(2,1)S(1)}, u32[]{:S(2)}, u32[]{:S(2)}) %collective-permute-start.15) | collective-permute-done | bytes 1572896 | tf_op jit(solution)/shard_map/ppermute | solution.py:8
  582.2 7.2 %maximum_select_fusion.11 = bf16[4096,384]{1,0:T(8,128)(2,1)S(1)} fusion(bf16[2048,384]{1,0:T(8,128)(2,1)S(1)} %maximum_select_fusion.14, bf16[2048,384]{1,0:T(8,128)(2,1)S(1)} %collective-permute-done.15, pred[]{:T(512)S(6)} %eq.15), kind=kLoop, calls=%fused_computation.41 | loop fusion | flops 14155776 | bytes 6291457 | tf_op jit(solution)/shard_map/jit(_where)/select_n | solution.py:34
  591.6 66.9 %collective-permute-done.16 = bf16[4096,384]{1,0:T(8,128)(2,1)S(1)} collective-permute-done((bf16[4096,384]{1,0:T(8,128)(2,1)S(1)}, bf16[4096,384]{1,0:T(8,128)(2,1)S(1)}, u32[]{:S(2)}, u32[]{:S(2)}) %collective-permute-start.16) | collective-permute-done | bytes 3145760 | tf_op jit(solution)/shard_map/ppermute | solution.py:8
  664.7 5.1 collective-permute-done.17
  (84 shorter events, 64.1 us)
Async XLA Ops:
  7.2 292.0 %copy-start = (bf16[128,8192]{1,0:T(8,128)(2,1)S(1)}, bf16[128,8192]{1,0:T(8,128)(2,1)}, u32[]{:S(2)}) copy-start(bf16[128,8192]{1,0:T(8,128)(2,1)} %param.20) | copy-start | bytes 6291460
  7.2 44.9 %all-gather.2.cloned.1.call-start = ((), (), s32[]{:S(2)}) async-start(), calls=%async_computation | async-start | bytes 1769472 | tf_op jit(solution)/shard_map/all_gather | solution.py:29
  52.1 3.8 collective-permute-start
  61.3 70.5 %collective-permute-start.1 = (bf16[4096,384]{1,0:T(8,128)(2,1)}, bf16[4096,384]{1,0:T(8,128)(2,1)}, u32[]{:S(2)}, u32[]{:S(2)}) collective-permute-start(bf16[4096,384]{1,0:T(8,128)(2,1)} %maximum_select_fusion.8), channel_id=1, source_target_pairs={{0,16},{8,24},{16,0},{24,8},{32,48},{40,56},{48,32},{56,40},{64,80... | collective-permute-start | bytes 9437192 | tf_op jit(solution)/shard_map/ppermute | solution.py:8
  140.8 11.9 %collective-permute-start.2 = (f32[256,384]{0,1:T(8,128)S(1)}, f32[256,384]{0,1:T(8,128)S(1)}, u32[]{:S(2)}, u32[]{:S(2)}) collective-permute-start(f32[256,384]{0,1:T(8,128)S(1)} %fusion.28), channel_id=1, source_target_pairs={{0,32},{8,40},{16,48},{24,56},{32,0},{40,8},{48,16},{56,24},{64,96... | collective-permute-start | bytes 1179656 | tf_op jit(solution)/shard_map/ppermute | solution.py:8
  180.5 2.3 collective-permute-start.3
  183.2 36.5 %collective-permute-start.4 = (bf16[2048,384]{1,0:T(8,128)(2,1)S(1)}, bf16[2048,384]{1,0:T(8,128)(2,1)S(1)}, u32[]{:S(2)}, u32[]{:S(2)}) collective-permute-start(bf16[2048,384]{1,0:T(8,128)(2,1)S(1)} %maximum_select_fusion.12), channel_id=1, source_target_pairs={{0,16},{8,24},{16,0},{24,8},{32,48},{40,56},{48,32},{56,40},{64,80... | collective-permute-start | bytes 4718600 | tf_op jit(solution)/shard_map/ppermute | solution.py:8
  228.0 71.1 %collective-permute-start.5 = (bf16[4096,384]{1,0:T(8,128)(2,1)}, bf16[4096,384]{1,0:T(8,128)(2,1)}, u32[]{:S(2)}, u32[]{:S(2)}) collective-permute-start(bf16[4096,384]{1,0:T(8,128)(2,1)} %maximum_select_fusion.9), channel_id=1, source_target_pairs={{0,32},{8,40},{16,48},{24,56},{32,0},{40,8},{48,16},{56,24},{64,96... | collective-permute-start | bytes 9437192 | tf_op jit(solution)/shard_map/ppermute | solution.py:8
  305.5 5.9 collective-permute-start.6
  338.4 1.7 collective-permute-start.7
  340.4 19.7 %collective-permute-start.8 = (bf16[1024,384]{1,0:T(8,128)(2,1)S(1)}, bf16[1024,384]{1,0:T(8,128)(2,1)S(1)}, u32[]{:S(2)}, u32[]{:S(2)}) collective-permute-start(bf16[1024,384]{1,0:T(8,128)(2,1)S(1)} %maximum_select_fusion.21), channel_id=1, source_target_pairs={{0,16},{8,24},{16,0},{24,8},{32,48},{40,56},{48,32},{56,40},{64,80... | collective-permute-start | bytes 2359304 | tf_op jit(solution)/shard_map/ppermute | solution.py:8
  360.5 114.2 %copy-start.6 = (bf16[64,8192]{1,0:T(8,128)(2,1)S(1)}, bf16[64,8192]{1,0:T(8,128)(2,1)}, u32[]{:S(2)}) copy-start(bf16[64,8192]{1,0:T(8,128)(2,1)} %param.21) | copy-start | bytes 3145732
  360.5 37.2 %collective-permute-start.9 = (bf16[2048,384]{1,0:T(8,128)(2,1)S(1)}, bf16[2048,384]{1,0:T(8,128)(2,1)S(1)}, u32[]{:S(2)}, u32[]{:S(2)}) collective-permute-start(bf16[2048,384]{1,0:T(8,128)(2,1)S(1)} %maximum_select_fusion.13), channel_id=1, source_target_pairs={{0,32},{8,40},{16,48},{24,56},{32,0},{40,8},{48,16},{56,24},{64,96... | collective-permute-start | bytes 4718600 | tf_op jit(solution)/shard_map/ppermute | solution.py:8
  406.0 68.7 %collective-permute-start.10 = (bf16[4096,384]{1,0:T(8,128)(2,1)}, bf16[4096,384]{1,0:T(8,128)(2,1)}, u32[]{:S(2)}, u32[]{:S(2)}) collective-permute-start(bf16[4096,384]{1,0:T(8,128)(2,1)} %maximum_select_fusion.10), channel_id=1, source_target_pairs={{0,64},{8,72},{16,80},{24,88},{32,96},{40,104},{48,112},{56,120},{... | collective-permute-start | bytes 9437192 | tf_op jit(solution)/shard_map/ppermute | solution.py:8
  480.9 6.2 collective-permute-start.11
  513.3 1.4 collective-permute-start.12
  514.9 11.2 %collective-permute-start.13 = (bf16[512,384]{1,0:T(8,128)(2,1)S(1)}, bf16[512,384]{1,0:T(8,128)(2,1)S(1)}, u32[]{:S(2)}, u32[]{:S(2)}) collective-permute-start(bf16[512,384]{1,0:T(8,128)(2,1)S(1)} %maximum_select_fusion.23), channel_id=1, source_target_pairs={{0,16},{8,24},{16,0},{24,8},{32,48},{40,56},{48,32},{56,40},{64,80... | collective-permute-start | bytes 1179656 | tf_op jit(solution)/shard_map/ppermute | solution.py:8
  526.4 20.3 %collective-permute-start.14 = (bf16[1024,384]{1,0:T(8,128)(2,1)S(1)}, bf16[1024,384]{1,0:T(8,128)(2,1)S(1)}, u32[]{:S(2)}, u32[]{:S(2)}) collective-permute-start(bf16[1024,384]{1,0:T(8,128)(2,1)S(1)} %maximum_select_fusion.22), channel_id=1, source_target_pairs={{0,32},{8,40},{16,48},{24,56},{32,0},{40,8},{48,16},{56,24},{64,96... | collective-permute-start | bytes 2359304 | tf_op jit(solution)/shard_map/ppermute | solution.py:8
  547.2 35.0 %collective-permute-start.15 = (bf16[2048,384]{1,0:T(8,128)(2,1)S(1)}, bf16[2048,384]{1,0:T(8,128)(2,1)S(1)}, u32[]{:S(2)}, u32[]{:S(2)}) collective-permute-start(bf16[2048,384]{1,0:T(8,128)(2,1)S(1)} %maximum_select_fusion.14), channel_id=1, source_target_pairs={{0,64},{8,72},{16,80},{24,88},{32,96},{40,104},{48,112},{56,120},{... | collective-permute-start | bytes 4718600 | tf_op jit(solution)/shard_map/ppermute | solution.py:8
  589.4 69.1 %collective-permute-start.16 = (bf16[4096,384]{1,0:T(8,128)(2,1)S(1)}, bf16[4096,384]{1,0:T(8,128)(2,1)S(1)}, u32[]{:S(2)}, u32[]{:S(2)}) collective-permute-start(bf16[4096,384]{1,0:T(8,128)(2,1)S(1)} %maximum_select_fusion.11), channel_id=1, source_target_pairs={{0,128},{8,136},{16,144},{24,152},{32,160},{40,168},{48,176},{56,1... | collective-permute-start | bytes 9437192 | tf_op jit(solution)/shard_map/ppermute | solution.py:8
  660.3 4.3 collective-permute-start.18
  662.3 7.5 %collective-permute-start.17 = (f32[2,1,16,384]{3,2,1,0:T(8,128)S(1)}, f32[2,1,16,384]{3,2,1,0:T(8,128)S(1)}, u32[]{:S(2)}, u32[]{:S(2)}) collective-permute-start(f32[2,1,16,384]{3,2,1,0:T(8,128)S(1)} %get-tuple-element.27), channel_id=1, source_target_pairs={{0,8},{8,16},{16,24},{24,32},{32,40},{40,48},{48,56},{56,64},{64,7... | collective-permute-start | bytes 147464 | tf_op jit(solution)/shard_map/ppermute | solution.py:19
  669.8 5.9 collective-permute-start.20
  673.1 5.6 collective-permute-start.19
  (6 other events, 300.0 us)
Sparse Core Ops, SparseCore 0:
  9.8 42.2 all-gather.1
where the time goes:
time: 687 us; the launch traced here: 686 us
  waiting for transfers between devices  498 us (72%)
  blocking collectives  75.7 us (11%)
  starting transfers between devices  35.3 us (5%)
  other arithmetic  32.4 us (5%)
  matrix products  23.4 us (3%)
  between operations  14.4 us (2%)
  local copies, waits for them, and re-layouts  6.91 us (1%)
    ppermute x17, waiting for transfers between devices, swapped(): lax.ppermute(x, axis, [(i, i ^ 1 << distance) for i in range(lax.axis_siz...  445 us
    all_gather x3, blocking collectives, group_rows(): values = lax.all_gather(values, 'gy', axis=0, tiled=True)  75.7 us
    all_gather x1, waiting for transfers between devices, group_rows(): values = lax.all_gather(values, 'gy', axis=0, tiled=True)  44.2 us
    select_n x10, other arithmetic, group_rows(): jnp.where(upper, jnp.concatenate([other, values], 0), jnp.concatenate([va...  31.2 us
    ppermute x17, starting transfers between devices, swapped(): lax.ppermute(x, axis, [(i, i ^ 1 << distance) for i in range(lax.axis_siz...  25.1 us
    dot_general x3, matrix products, local(): product = jnp.dot(fronts[level], whole, preferred_element_type=jnp.float32)  21.6 us
  transfers between devices with their start and end apart: 22, of which 20 were waited for; matrix products, arithmetic and copies ran while one was open for 0% of the time, Pallas kernels for 0%

commit v1 on v0

--- a/solution.py
+++ b/solution.py
@@ -26,7 +26,17 @@
 
 
 def group_rows(values, bits):
-    values = lax.all_gather(values, "gy", axis=0, tiled=True)
+
+    def edge_trace(q_in):
+        dev_n = lax.axis_size("gy")
+        all_blocks = []
+        for m in range(q_in.ndim):
+            all_blocks.append(dev_n if m == 0 else 1)
+        carry = jnp.tile(q_in, all_blocks)
+        even = lax.all_to_all(carry, "gy", split_axis=0, concat_axis=0, tiled=True)
+        return even
+
+    values = edge_trace(values)
     column = lax.axis_index("gx")
     for bit in range(bits):
         other = swapped(values, "gx", bit)

time: 687 us -> 652 us (0.949)
  waiting for transfers between devices: 498 us -> 452 us
  blocking collectives: 75.7 us -> 98.3 us
  between operations: 14.4 us -> 1 us
    all_to_all x0 -> x4, blocking collectives: none -> 98.3 us  [edge_trace(): even = lax.all_to_all(carry, 'gy', split_axis=0, concat_axis=0, tiled=True)]
    all_gather x3 -> x0, blocking collectives: 75.7 us -> none  [group_rows(): values = lax.all_gather(values, 'gy', axis=0, tiled=True)]
    all_gather x1 -> x0, waiting for transfers between devices: 44.2 us -> none  [group_rows(): values = lax.all_gather(values, 'gy', axis=0, tiled=True)]
  transfers between devices with their start and end apart: 22 -> 21, of which waited for: 20 -> 19; matrix products, arithmetic and copies ran while one was open for 0% -> 0% of each run, Pallas kernels for 0% -> 0%
where the time goes in v1:
time: 652 us
  waiting for transfers between devices  452 us (69%)
  blocking collectives  98.3 us (15%)
  starting transfers between devices  36.3 us (6%)
  other arithmetic  32.3 us (5%)
  matrix products  23.3 us (4%)
  local copies, waits for them, and re-layouts  8.24 us (1%)
    ppermute x17, waiting for transfers between devices, swapped(): lax.ppermute(x, axis, [(i, i ^ 1 << distance) for i in range(lax.axis_siz...  444 us
    all_to_all x4, blocking collectives, edge_trace(): even = lax.all_to_all(carry, 'gy', split_axis=0, concat_axis=0, tiled=True)  98.3 us
    select_n x10, other arithmetic, group_rows(): jnp.where(upper, jnp.concatenate([other, values], 0), jnp.concatenate([va...  31.1 us
    ppermute x17, starting transfers between devices, swapped(): lax.ppermute(x, axis, [(i, i ^ 1 << distance) for i in range(lax.axis_siz...  26.2 us
    dot_general x3, matrix products, local(): product = jnp.dot(fronts[level], whole, preferred_element_type=jnp.float32)  21.5 us
  transfers between devices with their start and end apart: 21, of which 19 were waited for; matrix products, arithmetic and copies ran while one was open for 0% of the time, Pallas kernels for 0%

profile of v1, /device:TPU:34, one launch (start us, length us, event | category | flops | bytes accessed | tf_op | source)
XLA Modules:
  0.0 651.8 jit_solution(12825064988890354405)
XLA Ops:
  1.9 47.0 %all_to_all.36 = bf16[8,256,384]{2,1,0:T(8,128)(2,1)} all-to-all(bf16[8,256,384]{2,1,0:T(8,128)(2,1)S(1)} %tile.8), channel_id=1, replica_groups=mesh['gx'=32,'gy'=8] {'gy'}, dimensions={0} | all-to-all | bytes 3145728 | tf_op jit(solution)/shard_map/all_to_all | solution.py:36
  52.6 5.4 maximum_select_fusion.8
  59.6 68.9 %collective-permute-done.1 = bf16[4096,384]{1,0:T(8,128)(2,1)} collective-permute-done((bf16[4096,384]{1,0:T(8,128)(2,1)}, bf16[4096,384]{1,0:T(8,128)(2,1)}, u32[]{:S(2)}, u32[]{:S(2)}) %collective-permute-start.1) | collective-permute-done | bytes 3145760 | tf_op jit(solution)/shard_map/ppermute | solution.py:8
  128.5 9.0 %fusion.28 = f32[256,384]{0,1:T(8,128)S(1)} fusion(bf16[256,8192]{1,0:T(8,128)(2,1)} %param.19, bf16[4096,384]{1,0:T(8,128)(2,1)} %maximum_select_fusion.8, bf16[4096,384]{1,0:T(8,128)(2,1)} %collective-permute-done.1, pred[]{:T(512)S(6)} %eq.17), kind=kOutput, calls=%fused_computation.45 | convolution fusion | flops 1638924288 | bytes 10878977 | tf_op jit(solution)/shard_map/dot_general | solution.py:74
  141.5 7.9 %collective-permute-done.2 = f32[256,384]{0,1:T(8,128)S(1)} collective-permute-done((f32[256,384]{0,1:T(8,128)S(1)}, f32[256,384]{0,1:T(8,128)S(1)}, u32[]{:S(2)}, u32[]{:S(2)}) %collective-permute-start.2) | collective-permute-done | bytes 393248 | tf_op jit(solution)/shard_map/ppermute | solution.py:8
  151.6 24.4 %all_to_all.37 = bf16[8,128,384]{2,1,0:T(8,128)(2,1)S(1)} all-to-all(bf16[8,128,384]{2,1,0:T(8,128)(2,1)S(1)} %tile.9), channel_id=1, replica_groups=mesh['gx'=32,'gy'=8] {'gy'}, dimensions={0} | all-to-all | bytes 1572864 | tf_op jit(solution)/shard_map/all_to_all | solution.py:36
  180.3 34.9 %collective-permute-done.4 = bf16[2048,384]{1,0:T(8,128)(2,1)S(1)} collective-permute-done((bf16[2048,384]{1,0:T(8,128)(2,1)S(1)}, bf16[2048,384]{1,0:T(8,128)(2,1)S(1)}, u32[]{:S(2)}, u32[]{:S(2)}) %collective-permute-start.4) | collective-permute-done | bytes 1572896 | tf_op jit(solution)/shard_map/ppermute | solution.py:8
  215.2 8.2 %maximum_select_fusion.9 = bf16[4096,384]{1,0:T(8,128)(2,1)} fusion(bf16[2048,384]{1,0:T(8,128)(2,1)S(1)} %maximum_select_fusion.12, bf16[2048,384]{1,0:T(8,128)(2,1)S(1)} %collective-permute-done.4, pred[]{:T(512)S(6)} %eq.17), kind=kLoop, calls=%fused_computation.39 | loop fusion | flops 14155776 | bytes 6291457 | tf_op jit(solution)/shard_map/jit(_where)/select_n | solution.py:44
  227.3 67.2 %collective-permute-done.5 = bf16[4096,384]{1,0:T(8,128)(2,1)} collective-permute-done((bf16[4096,384]{1,0:T(8,128)(2,1)}, bf16[4096,384]{1,0:T(8,128)(2,1)}, u32[]{:S(2)}, u32[]{:S(2)}) %collective-permute-start.5) | collective-permute-done | bytes 3145760 | tf_op jit(solution)/shard_map/ppermute | solution.py:8
  294.5 6.3 fusion.29
  301.7 5.1 collective-permute-done.6
  308.6 14.6 %all_to_all.38 = bf16[8,64,384]{2,1,0:T(8,128)(2,1)S(1)} all-to-all(bf16[8,64,384]{2,1,0:T(8,128)(2,1)S(1)} %tile.10), channel_id=1, replica_groups=mesh['gx'=32,'gy'=8] {'gy'}, dimensions={0} | all-to-all | bytes 786432 | tf_op jit(solution)/shard_map/all_to_all | solution.py:36
  326.8 18.0 %collective-permute-done.8 = bf16[1024,384]{1,0:T(8,128)(2,1)S(1)} collective-permute-done((bf16[1024,384]{1,0:T(8,128)(2,1)S(1)}, bf16[1024,384]{1,0:T(8,128)(2,1)S(1)}, u32[]{:S(2)}, u32[]{:S(2)}) %collective-permute-start.8) | collective-permute-done | bytes 786464 | tf_op jit(solution)/shard_map/ppermute | solution.py:8
  348.6 33.9 %collective-permute-done.9 = bf16[2048,384]{1,0:T(8,128)(2,1)S(1)} collective-permute-done((bf16[2048,384]{1,0:T(8,128)(2,1)S(1)}, bf16[2048,384]{1,0:T(8,128)(2,1)S(1)}, u32[]{:S(2)}, u32[]{:S(2)}) %collective-permute-start.9) | collective-permute-done | bytes 1572896 | tf_op jit(solution)/shard_map/ppermute | solution.py:8
  382.5 8.2 %maximum_select_fusion.10 = bf16[4096,384]{1,0:T(8,128)(2,1)} fusion(bf16[2048,384]{1,0:T(8,128)(2,1)S(1)} %maximum_select_fusion.13, bf16[2048,384]{1,0:T(8,128)(2,1)S(1)} %collective-permute-done.9, pred[]{:T(512)S(6)} %eq.16), kind=kLoop, calls=%fused_computation.40 | loop fusion | flops 14155776 | bytes 6291457 | tf_op jit(solution)/shard_map/jit(_where)/select_n | solution.py:44
  392.0 67.4 %collective-permute-done.10 = bf16[4096,384]{1,0:T(8,128)(2,1)} collective-permute-done((bf16[4096,384]{1,0:T(8,128)(2,1)}, bf16[4096,384]{1,0:T(8,128)(2,1)}, u32[]{:S(2)}, u32[]{:S(2)}) %collective-permute-start.10) | collective-permute-done | bytes 3145760 | tf_op jit(solution)/shard_map/ppermute | solution.py:8
  459.5 6.2 fusion.30
  473.2 12.4 %all_to_all.39 = bf16[8,32,384]{2,1,0:T(8,128)(2,1)S(1)} all-to-all(bf16[8,32,384]{2,1,0:T(8,128)(2,1)S(1)} %tile.11), channel_id=1, replica_groups=mesh['gx'=32,'gy'=8] {'gy'}, dimensions={0} | all-to-all | bytes 393216 | tf_op jit(solution)/shard_map/all_to_all | solution.py:36
  488.8 9.6 %collective-permute-done.13 = bf16[512,384]{1,0:T(8,128)(2,1)S(1)} collective-permute-done((bf16[512,384]{1,0:T(8,128)(2,1)S(1)}, bf16[512,384]{1,0:T(8,128)(2,1)S(1)}, u32[]{:S(2)}, u32[]{:S(2)}) %collective-permute-start.13) | collective-permute-done | bytes 393248 | tf_op jit(solution)/shard_map/ppermute | solution.py:8
  502.0 17.1 %collective-permute-done.14 = bf16[1024,384]{1,0:T(8,128)(2,1)S(1)} collective-permute-done((bf16[1024,384]{1,0:T(8,128)(2,1)S(1)}, bf16[1024,384]{1,0:T(8,128)(2,1)S(1)}, u32[]{:S(2)}, u32[]{:S(2)}) %collective-permute-start.14) | collective-permute-done | bytes 786464 | tf_op jit(solution)/shard_map/ppermute | solution.py:8
  520.3 34.2 %collective-permute-done.15 = bf16[2048,384]{1,0:T(8,128)(2,1)S(1)} collective-permute-done((bf16[2048,384]{1,0:T(8,128)(2,1)S(1)}, bf16[2048,384]{1,0:T(8,128)(2,1)S(1)}, u32[]{:S(2)}, u32[]{:S(2)}) %collective-permute-start.15) | collective-permute-done | bytes 1572896 | tf_op jit(solution)/shard_map/ppermute | solution.py:8
  554.5 7.2 %maximum_select_fusion.11 = bf16[4096,384]{1,0:T(8,128)(2,1)S(1)} fusion(bf16[2048,384]{1,0:T(8,128)(2,1)S(1)} %maximum_select_fusion.14, bf16[2048,384]{1,0:T(8,128)(2,1)S(1)} %collective-permute-done.15, pred[]{:T(512)S(6)} %eq.15), kind=kLoop, calls=%fused_computation.41 | loop fusion | flops 14155776 | bytes 6291457 | tf_op jit(solution)/shard_map/jit(_where)/select_n | solution.py:44
  563.9 66.9 %collective-permute-done.16 = bf16[4096,384]{1,0:T(8,128)(2,1)S(1)} collective-permute-done((bf16[4096,384]{1,0:T(8,128)(2,1)S(1)}, bf16[4096,384]{1,0:T(8,128)(2,1)S(1)}, u32[]{:S(2)}, u32[]{:S(2)}) %collective-permute-start.16) | collective-permute-done | bytes 3145760 | tf_op jit(solution)/shard_map/ppermute | solution.py:8
  637.0 5.1 collective-permute-done.17
  (86 shorter events, 65.9 us)
Async XLA Ops:
  0.6 293.9 %copy-start = (bf16[128,8192]{1,0:T(8,128)(2,1)S(1)}, bf16[128,8192]{1,0:T(8,128)(2,1)}, u32[]{:S(2)}) copy-start(bf16[128,8192]{1,0:T(8,128)(2,1)} %param.20) | copy-start | bytes 6291460
  48.8 3.8 collective-permute-start
  58.0 70.5 %collective-permute-start.1 = (bf16[4096,384]{1,0:T(8,128)(2,1)}, bf16[4096,384]{1,0:T(8,128)(2,1)}, u32[]{:S(2)}, u32[]{:S(2)}) collective-permute-start(bf16[4096,384]{1,0:T(8,128)(2,1)} %maximum_select_fusion.8), channel_id=1, source_target_pairs={{0,16},{8,24},{16,0},{24,8},{32,48},{40,56},{48,32},{56,40},{64,80... | collective-permute-start | bytes 9437192 | tf_op jit(solution)/shard_map/ppermute | solution.py:8
  137.5 11.9 %collective-permute-start.2 = (f32[256,384]{0,1:T(8,128)S(1)}, f32[256,384]{0,1:T(8,128)S(1)}, u32[]{:S(2)}, u32[]{:S(2)}) collective-permute-start(f32[256,384]{0,1:T(8,128)S(1)} %fusion.28), channel_id=1, source_target_pairs={{0,32},{8,40},{16,48},{24,56},{32,0},{40,8},{48,16},{56,24},{64,96... | collective-permute-start | bytes 1179656 | tf_op jit(solution)/shard_map/ppermute | solution.py:8
  175.9 2.3 collective-permute-start.3
  178.6 36.5 %collective-permute-start.4 = (bf16[2048,384]{1,0:T(8,128)(2,1)S(1)}, bf16[2048,384]{1,0:T(8,128)(2,1)S(1)}, u32[]{:S(2)}, u32[]{:S(2)}) collective-permute-start(bf16[2048,384]{1,0:T(8,128)(2,1)S(1)} %maximum_select_fusion.12), channel_id=1, source_target_pairs={{0,16},{8,24},{16,0},{24,8},{32,48},{40,56},{48,32},{56,40},{64,80... | collective-permute-start | bytes 4718600 | tf_op jit(solution)/shard_map/ppermute | solution.py:8
  223.4 71.1 %collective-permute-start.5 = (bf16[4096,384]{1,0:T(8,128)(2,1)}, bf16[4096,384]{1,0:T(8,128)(2,1)}, u32[]{:S(2)}, u32[]{:S(2)}) collective-permute-start(bf16[4096,384]{1,0:T(8,128)(2,1)} %maximum_select_fusion.9), channel_id=1, source_target_pairs={{0,32},{8,40},{16,48},{24,56},{32,0},{40,8},{48,16},{56,24},{64,96... | collective-permute-start | bytes 9437192 | tf_op jit(solution)/shard_map/ppermute | solution.py:8
  300.9 5.9 collective-permute-start.6
  323.1 1.7 collective-permute-start.7
  325.2 19.7 %collective-permute-start.8 = (bf16[1024,384]{1,0:T(8,128)(2,1)S(1)}, bf16[1024,384]{1,0:T(8,128)(2,1)S(1)}, u32[]{:S(2)}, u32[]{:S(2)}) collective-permute-start(bf16[1024,384]{1,0:T(8,128)(2,1)S(1)} %maximum_select_fusion.21), channel_id=1, source_target_pairs={{0,16},{8,24},{16,0},{24,8},{32,48},{40,56},{48,32},{56,40},{64,80... | collective-permute-start | bytes 2359304 | tf_op jit(solution)/shard_map/ppermute | solution.py:8
  345.3 114.2 %copy-start.6 = (bf16[64,8192]{1,0:T(8,128)(2,1)S(1)}, bf16[64,8192]{1,0:T(8,128)(2,1)}, u32[]{:S(2)}) copy-start(bf16[64,8192]{1,0:T(8,128)(2,1)} %param.21) | copy-start | bytes 3145732
  345.3 37.2 %collective-permute-start.9 = (bf16[2048,384]{1,0:T(8,128)(2,1)S(1)}, bf16[2048,384]{1,0:T(8,128)(2,1)S(1)}, u32[]{:S(2)}, u32[]{:S(2)}) collective-permute-start(bf16[2048,384]{1,0:T(8,128)(2,1)S(1)} %maximum_select_fusion.13), channel_id=1, source_target_pairs={{0,32},{8,40},{16,48},{24,56},{32,0},{40,8},{48,16},{56,24},{64,96... | collective-permute-start | bytes 4718600 | tf_op jit(solution)/shard_map/ppermute | solution.py:8
  390.7 68.7 %collective-permute-start.10 = (bf16[4096,384]{1,0:T(8,128)(2,1)}, bf16[4096,384]{1,0:T(8,128)(2,1)}, u32[]{:S(2)}, u32[]{:S(2)}) collective-permute-start(bf16[4096,384]{1,0:T(8,128)(2,1)} %maximum_select_fusion.10), channel_id=1, source_target_pairs={{0,64},{8,72},{16,80},{24,88},{32,96},{40,104},{48,112},{56,120},{... | collective-permute-start | bytes 9437192 | tf_op jit(solution)/shard_map/ppermute | solution.py:8
  465.6 6.2 collective-permute-start.11
  485.6 1.4 collective-permute-start.12
  487.2 11.2 %collective-permute-start.13 = (bf16[512,384]{1,0:T(8,128)(2,1)S(1)}, bf16[512,384]{1,0:T(8,128)(2,1)S(1)}, u32[]{:S(2)}, u32[]{:S(2)}) collective-permute-start(bf16[512,384]{1,0:T(8,128)(2,1)S(1)} %maximum_select_fusion.23), channel_id=1, source_target_pairs={{0,16},{8,24},{16,0},{24,8},{32,48},{40,56},{48,32},{56,40},{64,80... | collective-permute-start | bytes 1179656 | tf_op jit(solution)/shard_map/ppermute | solution.py:8
  498.7 20.3 %collective-permute-start.14 = (bf16[1024,384]{1,0:T(8,128)(2,1)S(1)}, bf16[1024,384]{1,0:T(8,128)(2,1)S(1)}, u32[]{:S(2)}, u32[]{:S(2)}) collective-permute-start(bf16[1024,384]{1,0:T(8,128)(2,1)S(1)} %maximum_select_fusion.22), channel_id=1, source_target_pairs={{0,32},{8,40},{16,48},{24,56},{32,0},{40,8},{48,16},{56,24},{64,96... | collective-permute-start | bytes 2359304 | tf_op jit(solution)/shard_map/ppermute | solution.py:8
  519.5 111.3 %copy-start.7 = (bf16[32,8192]{1,0:T(8,128)(2,1)S(1)}, bf16[32,8192]{1,0:T(8,128)(2,1)}, u32[]{:S(2)}) copy-start(bf16[32,8192]{1,0:T(8,128)(2,1)} %param.22) | copy-start | bytes 1572868
  519.5 35.0 %collective-permute-start.15 = (bf16[2048,384]{1,0:T(8,128)(2,1)S(1)}, bf16[2048,384]{1,0:T(8,128)(2,1)S(1)}, u32[]{:S(2)}, u32[]{:S(2)}) collective-permute-start(bf16[2048,384]{1,0:T(8,128)(2,1)S(1)} %maximum_select_fusion.14), channel_id=1, source_target_pairs={{0,64},{8,72},{16,80},{24,88},{32,96},{40,104},{48,112},{56,120},{... | collective-permute-start | bytes 4718600 | tf_op jit(solution)/shard_map/ppermute | solution.py:8
  561.7 69.1 %collective-permute-start.16 = (bf16[4096,384]{1,0:T(8,128)(2,1)S(1)}, bf16[4096,384]{1,0:T(8,128)(2,1)S(1)}, u32[]{:S(2)}, u32[]{:S(2)}) collective-permute-start(bf16[4096,384]{1,0:T(8,128)(2,1)S(1)} %maximum_select_fusion.11), channel_id=1, source_target_pairs={{0,128},{8,136},{16,144},{24,152},{32,160},{40,168},{48,176},{56,1... | collective-permute-start | bytes 9437192 | tf_op jit(solution)/shard_map/ppermute | solution.py:8
  632.6 4.3 collective-permute-start.18
  634.6 7.5 %collective-permute-start.17 = (f32[2,1,16,384]{3,2,1,0:T(8,128)S(1)}, f32[2,1,16,384]{3,2,1,0:T(8,128)S(1)}, u32[]{:S(2)}, u32[]{:S(2)}) collective-permute-start(f32[2,1,16,384]{3,2,1,0:T(8,128)S(1)} %get-tuple-element.27), channel_id=1, source_target_pairs={{0,8},{8,16},{16,24},{24,32},{32,40},{40,48},{48,56},{56,64},{64,7... | collective-permute-start | bytes 147464 | tf_op jit(solution)/shard_map/ppermute | solution.py:19
  642.1 5.9 collective-permute-start.20
  645.5 5.6 collective-permute-start.19
  (5 other events, 188.6 us)
